TPU v7x, 32 devices: a whole 2x2x4 slice. The times are simulated.
32 devices in a mesh: illum: 8 (over z, y), tile: 4 (over x, core).
Axes of the slice: x: 2, y: 2, z: 4, core: 2. Of those that a mesh axis runs over, the one named last changes fastest.
Arguments:
- tilts: int32 [8, 2], P('illum'), may hold values from -64 to 64
- taps: float32 [2, 33], replicated, may hold values from -0.75 to 0.75
- stored_planes: float32 [2, 128, 4096], P(None, 'tile', 'illum'), may hold values from -3.140625 to 3.140625
- owner: int32 [2, 8], replicated, may hold values from 0 to 7, each once within a row
Outputs:
- exit_field: float32 [2, 8, 128, 4096], P(None, 'illum', 'tile')
Inputs may be any that keep to these rules, and one draw needn't show every extreme that they name: Each row of owner is a permutation of the 8 stored column blocks.
All inputs are finite; a program needn't handle non-finite values.
Results may differ from a plain program's by a relative error of at most 0.0003.
Values sent between devices are 32-bit elements; how exact they have to be, the bound alone decides.
No kernel may reach another device: no remote copies, remote signals or barrier semaphores. Data moves between devices by JAX's collectives and lax.ppermute only.
A program may use at most 64 MiB of HBM per device.

v0:
```python
import jax
import jax.numpy as jnp
from jax import lax
from jax.sharding import PartitionSpec as P

NY = 4096
PLANES = 2
HALF = 16
two_pi = 6.283185307179586


def extended(cells, sides, width):
    for axis, dim in sides:
        count = lax.axis_size(axis)
        ends = count - 1
        head = lax.slice_in_dim(cells, 0, width, axis=dim)
        tail = lax.slice_in_dim(cells, cells.shape[dim] - width, cells.shape[dim], axis=dim)
        cells = jnp.concatenate(
            [
                lax.ppermute(tail, axis, [(i, (i + 1) % count) for i in range(ends)]),
                cells,
                lax.ppermute(head, axis, [((i + 1) % count, i) for i in range(ends)]),
            ],
            axis=dim,
        )
    return cells


def toeplitz(tap_row, block):
    rows = jnp.arange(block + 2 * HALF)[:, None]
    cols = jnp.arange(block)[None, :]
    offset = rows - cols
    steps = jnp.arange(2 * HALF + 1)
    return jnp.sum(jnp.where(offset[:, :, None] == steps, tap_row, 0.0), axis=2)


def band_matrix(tap_row, count):
    rows = jnp.arange(count)[:, None]
    cols = jnp.arange(count + 2 * HALF)[None, :]
    offset = cols - rows
    steps = jnp.arange(2 * HALF + 1)
    return jnp.sum(jnp.where(offset[:, :, None] == steps, tap_row, 0.0), axis=2)


def windows(field, block):
    length = field.shape[-1]
    count = length // block
    widths = [(0, 0)] * (field.ndim - 1) + [(HALF, block - HALF)]
    padded = jnp.pad(field, widths)
    lead = field.shape[:-1]
    main = padded[..., :length].reshape(lead + (count, block))
    after = padded[..., block : length + block].reshape(lead + (count, block))[..., : 2 * HALF]
    return jnp.concatenate([main, after], axis=-1)


def along_pass(real, imag, taps):
    block = min(128, real.shape[-1])
    win_real = windows(real, block)
    win_imag = windows(imag, block)
    kern_real = toeplitz(taps[0], block)
    kern_imag = toeplitz(taps[1], block)

    def apply(win, kern):
        out = jnp.einsum("...nj,jc->...nc", win, kern, precision=lax.Precision.HIGHEST)
        return out.reshape(real.shape)

    return (
        apply(win_real, kern_real) - apply(win_imag, kern_imag),
        apply(win_real, kern_imag) + apply(win_imag, kern_real),
    )


def cross_pass(real, imag, taps):
    count = real.shape[1] - 2 * HALF
    band_real = band_matrix(taps[0], count)
    band_imag = band_matrix(taps[1], count)

    def apply(band, field):
        return jnp.einsum("ij,ajy->aiy", band, field, precision=lax.Precision.HIGHEST)

    return (
        apply(band_real, real) - apply(band_imag, imag),
        apply(band_real, imag) + apply(band_imag, real),
    )


def transmit(real, imag, screen):
    cosine = jnp.cos(screen)
    sine = jnp.sin(screen)
    return (real * cosine - imag * sine, real * sine + imag * cosine)


def reorder(gathered, owner):
    count = gathered.shape[1]
    blocks = owner.shape[1]
    width = gathered.shape[2] // blocks
    planes = [
        gathered[p].reshape(count, blocks, width)[:, owner[p], :].reshape(count, blocks * width)
        for p in range(gathered.shape[0])
    ]
    return jnp.stack(planes)


def body(tilts, taps, stored_planes, owner):
    local_rows = stored_planes.shape[1]
    total_rows = local_rows * lax.axis_size("tile")
    total_cols = NY
    first_row = lax.axis_index("tile") * local_rows
    gathered = lax.all_gather(stored_planes, "illum", axis=2, tiled=True)
    screens = reorder(gathered, owner)
    extra = 0
    span = local_rows + 2 * extra
    global_rows = first_row - extra + jnp.arange(span, dtype=jnp.int32)
    inside = (global_rows >= 0) & (global_rows < total_rows)
    cols = jnp.arange(total_cols, dtype=jnp.int32)
    across = (
        jnp.mod(tilts[:, 0:1] * global_rows[None, :], total_rows).astype(jnp.float32) / total_rows
    )
    along = jnp.mod(tilts[:, 1:2] * cols[None, :], total_cols).astype(jnp.float32) / total_cols
    theta = two_pi * (across[:, :, None] + along[:, None, :])
    real = jnp.where(inside[None, :, None], jnp.cos(theta), 0.0)
    imag = jnp.where(inside[None, :, None], jnp.sin(theta), 0.0)
    for plane in range(PLANES):
        real, imag = transmit(real, imag, screens[plane])
        packed = extended(jnp.stack([real, imag]), (("tile", 2),), HALF)
        real, imag = cross_pass(packed[0], packed[1], taps)
        real, imag = along_pass(real, imag, taps)
    return jnp.stack([real, imag])


def solution(mesh):
    in_specs = (P("illum", None), P(), P(None, "tile", "illum"), P())
    out_specs = P(None, "illum", "tile", None)
    return jax.shard_map(body, mesh=mesh, in_specs=in_specs, out_specs=out_specs, check_vma=False)
```

profile of v0, /device:TPU:1, one launch (start us, length us, event | category | flops | bytes accessed | tf_op | source)
XLA Modules:
  0.0 116.0 jit_solution(4339684245039347680)
XLA Ops:
  6.5 0.7 all-gather.2.cloned.1.call-update
  7.3 1.4 %fusion.42 = (s32[1,1]{1,0:T(1,128)}, s32[1,1]{1,0:T(1,128)}) fusion(s32[1,2]{1,0:T(1,128)} %param.4), kind=kLoop, calls=%fused_computation.110 | loop fusion | bytes 16 | tf_op jit(solution)/shard_map/slice | solution.py:117
  8.7 0.7 fusion.29
  9.3 0.8 fusion.32
  10.1 0.7 fusion.24
  10.8 0.8 slice_bitcast_fusion.20
  11.6 0.2 select_reduce_fusion.3
  11.8 39.1 %all-gather.2.cloned.1.call-done = f32[2,32,4096]{2,1,0:T(8,128)} async-done(((f32[2,32,512]{2,1,0:T(8,128)}), f32[2,32,4096]{2,1,0:T(8,128)}) %all-gather.2.cloned.1.call-update) | async-done | bytes 1048592 | tf_op jit(solution)/shard_map/all_gather | solution.py:109
  50.9 1.3 %fusion.41 = (f32[1,32,4096]{2,1,0:T(8,128)S(1)}, f32[1,32,4096]{2,1,0:T(8,128)S(1)}) fusion(f32[2,32,4096]{2,1,0:T(8,128)} %all-gather.2.cloned.1.call-done), kind=kLoop, calls=%fused_computation.109 | loop fusion | bytes 2097152 | tf_op jit(solution)/shard_map/slice | solution.py:98
  52.1 0.3 copy.17
  52.5 0.3 copy.11
  52.8 0.6 gather_fusion
  53.4 1.9 %sine_bitcast_fusion.1 = (f32[32,8,512]{2,0,1:T(8,128)S(1)}, f32[32,8,512]{2,0,1:T(8,128)S(1)}) fusion(f32[8,32,512]{2,1,0:T(8,128)S(1)} %gather_fusion), kind=kLoop, calls=%fused_computation.49 | loop fusion | bytes 1572864 | tf_op jit(solution)/shard_map/sin | solution.py:89
  55.2 0.3 copy.12
  55.5 0.1 cos.57
  55.6 0.3 copy.13
  56.0 0.1 sin.57
  56.1 2.2 %multiply_subtract_fusion.1 = (f32[1,1,32,4096]{3,2,1,0:T(8,128)S(1)}, f32[1,1,32,4096]{3,2,1,0:T(8,128)S(1)}) fusion(f32[1,1,32,4096]{3,2,1,0:T(8,128)S(1)} %sin.57, f32[1,1,32,4096]{3,2,1,0:T(8,128)S(1)} %cos.57, f32[4096]{0:T(1024)S(1)} %fusion.24, f32[32]{0:T(128)S(1)} %fusion.29, pred[32]{0:T(512)(128)(4,1)S(1)} %compare_and_fusion), kind=kLoop, calls=%fused_computation.62 | loop fusion | flops 1310720 | bytes 2113696 | tf_op jit(solution)/shard_map/sub | solution.py:90
  58.2 0.9 fusion.13
  59.1 4.6 %collective-permute-start = (f32[2,1,16,4096]{3,2,1,0:T(8,128)}, f32[2,1,16,4096]{3,2,1,0:T(8,128)}, u32[]{:S(2)}, u32[]{:S(2)}) collective-permute-start(f32[2,1,16,4096]{3,2,1,0:T(8,128)} %get-tuple-element.17), channel_id=1, source_target_pairs={{0,1},{1,2},{2,3},{4,5},{5,6},{6,7},{8,9},{9,10},{10,11},{12,13},{... | collective-permute-start | bytes 1572872 | tf_op jit(solution)/shard_map/ppermute | solution.py:20
  63.8 2.1 %collective-permute-start.1 = (f32[2,1,16,4096]{3,2,1,0:T(8,128)S(1)}, f32[2,1,16,4096]{3,2,1,0:T(8,128)}, u32[]{:S(2)}, u32[]{:S(2)}) collective-permute-start(f32[2,1,16,4096]{3,2,1,0:T(8,128)S(1)} %get-tuple-element.18), channel_id=1, source_target_pairs={{1,0},{2,1},{3,2},{5,4},{6,5},{7,6},{9,8},{10,9},{11,10},{13,12},{... | collective-permute-start | bytes 1572872 | tf_op jit(solution)/shard_map/ppermute | solution.py:22
  65.9 0.6 select_reduce_fusion.1
  66.4 0.3 copy.22
  66.8 0.3 copy.14
  67.1 0.6 gather_fusion.1
  67.7 1.9 %sine_bitcast_fusion = (f32[32,8,512]{2,0,1:T(8,128)S(1)}, f32[32,8,512]{2,0,1:T(8,128)S(1)}) fusion(f32[8,32,512]{2,1,0:T(8,128)S(1)} %gather_fusion.1), kind=kLoop, calls=%fused_computation.47 | loop fusion | bytes 1572864 | tf_op jit(solution)/shard_map/sin | solution.py:89
  69.5 0.3 copy.15
  69.9 0.1 cos.59
  70.0 0.3 copy.16
  70.3 0.1 sin.59
  70.4 4.0 %collective-permute-done.1 = f32[2,1,16,4096]{3,2,1,0:T(8,128)} collective-permute-done((f32[2,1,16,4096]{3,2,1,0:T(8,128)S(1)}, f32[2,1,16,4096]{3,2,1,0:T(8,128)}, u32[]{:S(2)}, u32[]{:S(2)}) %collective-permute-start.1) | collective-permute-done | bytes 524320 | tf_op jit(solution)/shard_map/ppermute | solution.py:22
  74.4 1.3 %pad_maximum_fusion = f32[2,1,64,4096]{3,2,1,0:T(8,128)S(1)} fusion(f32[2,1,16,4096]{3,2,1,0:T(8,128)} %collective-permute-done.1, f32[1,1,32,4096]{3,2,1,0:T(8,128)S(1)} %get-tuple-element.12, f32[1,1,32,4096]{3,2,1,0:T(8,128)S(1)} %get-tuple-element.11, f32[2,1,16,4096]{3,2,1,0:T(8,128)} %collective-permute-done), kind=kLoop, calls=%fused_computation.13 | loop fusion | flops 1572864 | bytes 4194304 | tf_op jit(solution)/shard_map/concatenate | solution.py:18
  75.7 0.7 fusion.5
  76.4 0.7 fusion.4
  77.1 0.7 fusion
  77.8 0.3 slice_bitcast_fusion.19
  78.2 0.1 copy.18
  78.3 0.7 fusion.1
  79.0 0.3 slice_bitcast_fusion.17
  79.6 1.0 fusion.11
  80.5 1.0 fusion.10
  81.5 1.8 %convolution_subtract_fusion.3 = f32[32,32,128]{2,1,0:T(8,128)} fusion(f32[32,32,128]{2,1,0:T(8,128)S(1)} %fusion.11, f32[1,32,32,32]{3,2,1,0:T(8,128)S(1)} %bitcast.154, f32[1,32,32,128]{3,2,1,0:T(8,128)S(1)} %bitcast.156, f32[160,128]{1,0:T(8,128)S(1)} %get-tuple-element.6), kind=kOutput, calls=%fused_computation.18 | convolution fusion | flops 251953152 | bytes 1785856 | tf_op jit(solution)/shard_map/...nj,jc->...nc/dot_general | solution.py:64
  83.3 1.1 sub.176
  84.4 1.8 %convolution_add_fusion.3 = f32[32,32,128]{2,1,0:T(8,128)} fusion(f32[32,32,128]{2,1,0:T(8,128)S(1)} %fusion.10, f32[1,32,32,32]{3,2,1,0:T(8,128)S(1)} %bitcast.155, f32[1,32,32,128]{3,2,1,0:T(8,128)S(1)} %bitcast.157, f32[160,128]{1,0:T(8,128)S(1)} %get-tuple-element.5), kind=kOutput, calls=%fused_computation.17 | convolution fusion | flops 251953152 | bytes 1785856 | tf_op jit(solution)/shard_map/...nj,jc->...nc/dot_general | solution.py:64
  86.2 1.1 add.184
  87.3 0.1 multiply_subtract_fusion
  87.5 1.9 %collective-permute-start.2 = (f32[2,1,16,4096]{3,2,1,0:T(8,128)S(1)}, f32[2,1,16,4096]{3,2,1,0:T(8,128)S(1)}, u32[]{:S(2)}, u32[]{:S(2)}) collective-permute-start(f32[2,1,16,4096]{3,2,1,0:T(8,128)S(1)} %get-tuple-element.13), channel_id=1, source_target_pairs={{0,1},{1,2},{2,3},{4,5},{5,6},{6,7},{8,9},{9,10},{10,11},{12,13},{... | collective-permute-start | bytes 1572872 | tf_op jit(solution)/shard_map/ppermute | solution.py:20
  89.5 2.7 %collective-permute-start.3 = (f32[2,1,16,4096]{3,2,1,0:T(8,128)S(1)}, f32[2,1,16,4096]{3,2,1,0:T(8,128)S(1)}, u32[]{:S(2)}, u32[]{:S(2)}) collective-permute-start(f32[2,1,16,4096]{3,2,1,0:T(8,128)S(1)} %get-tuple-element.14), channel_id=1, source_target_pairs={{1,0},{2,1},{3,2},{5,4},{6,5},{7,6},{9,8},{10,9},{11,10},{13,12},{... | collective-permute-start | bytes 1572872 | tf_op jit(solution)/shard_map/ppermute | solution.py:22
  92.1 3.4 %collective-permute-done.2 = f32[2,1,16,4096]{3,2,1,0:T(8,128)S(1)} collective-permute-done((f32[2,1,16,4096]{3,2,1,0:T(8,128)S(1)}, f32[2,1,16,4096]{3,2,1,0:T(8,128)S(1)}, u32[]{:S(2)}, u32[]{:S(2)}) %collective-permute-start.2) | collective-permute-done | bytes 524320 | tf_op jit(solution)/shard_map/ppermute | solution.py:20
  95.6 4.4 %collective-permute-done.3 = f32[2,1,16,4096]{3,2,1,0:T(8,128)S(1)} collective-permute-done((f32[2,1,16,4096]{3,2,1,0:T(8,128)S(1)}, f32[2,1,16,4096]{3,2,1,0:T(8,128)S(1)}, u32[]{:S(2)}, u32[]{:S(2)}) %collective-permute-start.3) | collective-permute-done | bytes 524320 | tf_op jit(solution)/shard_map/ppermute | solution.py:22
  100.0 0.2 pad_maximum_fusion.1
  100.2 0.7 fusion.7
  100.8 0.7 fusion.6
  101.5 0.7 fusion.2
  102.2 0.3 slice_bitcast_fusion.15
  102.8 1.0 fusion.9
  103.7 1.0 fusion.8
  104.7 0.7 fusion.3
  105.4 0.3 slice_bitcast_fusion.13
  105.9 1.0 convolution_subtract_fusion.2
  106.9 0.1 sub.182
  107.0 1.0 convolution_add_fusion.2
  108.0 0.1 add.190
  108.1 1.0 pad_maximum_fusion.2
  (14 shorter events, 0.8 us)
Async XLA Ops:
  6.5 44.3 %all-gather.2.cloned.1.call-start = ((), (), s32[]{:S(2)}) async-start(), calls=%async_computation | async-start | bytes 1179648 | tf_op jit(solution)/shard_map/all_gather | solution.py:109
  59.1 11.3 %collective-permute-start = (f32[2,1,16,4096]{3,2,1,0:T(8,128)}, f32[2,1,16,4096]{3,2,1,0:T(8,128)}, u32[]{:S(2)}, u32[]{:S(2)}) collective-permute-start(f32[2,1,16,4096]{3,2,1,0:T(8,128)} %get-tuple-element.17), channel_id=1, source_target_pairs={{0,1},{1,2},{2,3},{4,5},{5,6},{6,7},{8,9},{9,10},{10,11},{12,13},{... | collective-permute-start | bytes 1572872 | tf_op jit(solution)/shard_map/ppermute | solution.py:20
  63.8 10.6 %collective-permute-start.1 = (f32[2,1,16,4096]{3,2,1,0:T(8,128)S(1)}, f32[2,1,16,4096]{3,2,1,0:T(8,128)}, u32[]{:S(2)}, u32[]{:S(2)}) collective-permute-start(f32[2,1,16,4096]{3,2,1,0:T(8,128)S(1)} %get-tuple-element.18), channel_id=1, source_target_pairs={{1,0},{2,1},{3,2},{5,4},{6,5},{7,6},{9,8},{10,9},{11,10},{13,12},{... | collective-permute-start | bytes 1572872 | tf_op jit(solution)/shard_map/ppermute | solution.py:22
  87.5 8.0 %collective-permute-start.2 = (f32[2,1,16,4096]{3,2,1,0:T(8,128)S(1)}, f32[2,1,16,4096]{3,2,1,0:T(8,128)S(1)}, u32[]{:S(2)}, u32[]{:S(2)}) collective-permute-start(f32[2,1,16,4096]{3,2,1,0:T(8,128)S(1)} %get-tuple-element.13), channel_id=1, source_target_pairs={{0,1},{1,2},{2,3},{4,5},{5,6},{6,7},{8,9},{9,10},{10,11},{12,13},{... | collective-permute-start | bytes 1572872 | tf_op jit(solution)/shard_map/ppermute | solution.py:20
  89.5 10.5 %collective-permute-start.3 = (f32[2,1,16,4096]{3,2,1,0:T(8,128)S(1)}, f32[2,1,16,4096]{3,2,1,0:T(8,128)S(1)}, u32[]{:S(2)}, u32[]{:S(2)}) collective-permute-start(f32[2,1,16,4096]{3,2,1,0:T(8,128)S(1)} %get-tuple-element.14), channel_id=1, source_target_pairs={{1,0},{2,1},{3,2},{5,4},{6,5},{7,6},{9,8},{10,9},{11,10},{13,12},{... | collective-permute-start | bytes 1572872 | tf_op jit(solution)/shard_map/ppermute | solution.py:22
Sparse Core Ops, SparseCore 0:
  9.5 41.2 all-gather.1
where the time goes:
time: 116 us
  waiting for transfers between devices  51.6 us (44%)
  local copies, waits for them, and re-layouts  15.7 us (14%)
  matrix products  14.8 us (13%)
  between operations  13.8 us (12%)
  starting transfers between devices  11.3 us (10%)
  other arithmetic  8.69 us (7%)
    all_gather x1, waiting for transfers between devices, body(): gathered = lax.all_gather(stored_planes, 'illum', axis=2, tiled=True)  39.1 us
    dot_general x8, matrix products, apply(): jnp.einsum('...nj,jc->...nc', win, kern, precision=lax.Precision.HIGHEST)  9.36 us
    ppermute x2, waiting for transfers between devices, extended(): lax.ppermute(head, axis, [((i + 1) % count, i) for i in range(ends)])  8.37 us
    ppermute x2, starting transfers between devices, extended(): lax.ppermute(tail, axis, [(i, (i + 1) % count) for i in range(ends)])  6.56 us
    dot_general x8, matrix products, apply(): jnp.einsum('ij,ajy->aiy', band, field, precision=lax.Precision.HIGHEST)  5.44 us
    ppermute x2, starting transfers between devices, extended(): lax.ppermute(head, axis, [((i + 1) % count, i) for i in range(ends)])  4.76 us
    sin x6, local copies, waits for them, and re-layouts, transmit(): sine = jnp.sin(screen)  4.53 us
    ppermute x2, waiting for transfers between devices, extended(): lax.ppermute(tail, axis, [(i, (i + 1) % count) for i in range(ends)])  3.44 us
  transfers between devices with their start and end apart: 5, of which 4 were waited for; matrix products, arithmetic and copies ran while one was open for 8% of the time, Pallas kernels for 0%

commit v1 on v0

--- a/solution.py
+++ b/solution.py
@@ -106,7 +106,15 @@
     total_rows = local_rows * lax.axis_size("tile")
     total_cols = NY
     first_row = lax.axis_index("tile") * local_rows
-    gathered = lax.all_gather(stored_planes, "illum", axis=2, tiled=True)
+    ways, here, hop = (lax.axis_size("illum"), lax.axis_index("illum"), stored_planes.shape[2])
+    line, have = (stored_planes, 1)
+    while have < ways:
+        line = jnp.concatenate(
+            [line, lax.ppermute(line, "illum", [(d, (d - have) % ways) for d in range(ways)])],
+            axis=2,
+        )
+        have = 2 * have
+    gathered = jnp.roll(line, here * hop, axis=2)
     screens = reorder(gathered, owner)
     extra = 0
     span = local_rows + 2 * extra

time: 116 us -> 99.2 us (0.86)
  between operations: 13.8 us -> 0.53 us
  waiting for transfers between devices: 51.6 us -> 40.5 us
  starting transfers between devices: 11.3 us -> 16.5 us
  other arithmetic: 8.69 us -> 10.4 us
    all_gather x1 -> x0, waiting for transfers between devices: 39.1 us -> none  [body(): gathered = lax.all_gather(stored_planes, 'illum', axis=2, tiled=True)]
    ppermute x0 -> x3, waiting for transfers between devices: none -> 28.7 us  [body(): lax.ppermute(line, 'illum', [(d, (d - have) % ways) for d in range(ways)])]
    ppermute x0 -> x3, starting transfers between devices: none -> 6.17 us  [body(): lax.ppermute(line, 'illum', [(d, (d - have) % ways) for d in range(ways)])]
    concatenate x0 -> x2, other arithmetic: none -> 1.86 us  [body(): jnp.concatenate([line, lax.ppermute(line, 'illum', [(d, (d - have) % ways...]
    slice x1, local copies, waits for them, and re-layouts: 1.27 us -> 0.08 us  [reorder(): gathered[p].reshape(count, blocks, width)[:, owner[p], :]]
    unnamed x14 -> x23, local copies, waits for them, and re-layouts: 2.72 us -> 3.75 us
  transfers between devices with their start and end apart: 5 -> 7, of which waited for: 4 -> 5; matrix products, arithmetic and copies ran while one was open for 8% -> 10% of each run, Pallas kernels for 0% -> 0%
where the time goes in v1:
time: 99.2 us; the launch traced here: 98.3 us
  waiting for transfers between devices  40.5 us (41%)
  starting transfers between devices  16.5 us (17%)
  local copies, waits for them, and re-layouts  15.5 us (16%)
  matrix products  14.8 us (15%)
  other arithmetic  10.4 us (10%)
    ppermute x3, waiting for transfers between devices, body(): lax.ppermute(line, 'illum', [(d, (d - have) % ways) for d in range(ways)])  28.7 us
    dot_general x8, matrix products, apply(): jnp.einsum('...nj,jc->...nc', win, kern, precision=lax.Precision.HIGHEST)  9.37 us
    ppermute x2, waiting for transfers between devices, extended(): lax.ppermute(head, axis, [((i + 1) % count, i) for i in range(ends)])  8.37 us
    ppermute x3, starting transfers between devices, body(): lax.ppermute(line, 'illum', [(d, (d - have) % ways) for d in range(ways)])  6.17 us
    ppermute x2, starting transfers between devices, extended(): lax.ppermute(tail, axis, [(i, (i + 1) % count) for i in range(ends)])  5.58 us
    dot_general x8, matrix products, apply(): jnp.einsum('ij,ajy->aiy', band, field, precision=lax.Precision.HIGHEST)  5.44 us
    ppermute x2, starting transfers between devices, extended(): lax.ppermute(head, axis, [((i + 1) % count, i) for i in range(ends)])  4.76 us
    sin x6, local copies, waits for them, and re-layouts, transmit(): sine = jnp.sin(screen)  4.53 us
  transfers between devices with their start and end apart: 7, of which 5 were waited for; matrix products, arithmetic and copies ran while one was open for 10% of the time, Pallas kernels for 0%

profile of v1, /device:TPU:1, one launch (start us, length us, event | category | flops | bytes accessed | tf_op | source)
XLA Modules:
  0.0 98.3 jit_solution(3632952811798959521)
XLA Ops:
  0.0 5.1 %collective-permute-start = (f32[2,32,512]{2,1,0:T(8,128)}, f32[2,32,512]{2,1,0:T(8,128)S(1)}, u32[]{:S(2)}, u32[]{:S(2)}) collective-permute-start(f32[2,32,512]{2,1,0:T(8,128)} %param.6), channel_id=1, source_target_pairs={{0,28},{4,0},{8,4},{12,8},{16,12},{20,16},{24,20},{28,24},{1,29},{... | collective-permute-start | bytes 393224 | tf_op jit(solution)/shard_map/ppermute | solution.py:113
  5.1 0.8 fusion.32
  5.9 1.3 %fusion.41 = (s32[1,1]{1,0:T(1,128)}, s32[1,1]{1,0:T(1,128)}) fusion(s32[1,2]{1,0:T(1,128)} %param.4), kind=kLoop, calls=%fused_computation.121 | loop fusion | bytes 16 | tf_op jit(solution)/shard_map/slice | solution.py:125
  7.2 0.6 fusion.24
  7.8 0.9 pad_maximum_fusion.6
  8.7 1.0 %collective-permute-start.1 = (f32[2,32,1024]{2,1,0:T(8,128)S(1)}, f32[2,32,1024]{2,1,0:T(8,128)S(1)}, u32[]{:S(2)}, u32[]{:S(2)}) collective-permute-start(f32[2,32,1024]{2,1,0:T(8,128)S(1)} %pad_maximum_fusion.6), channel_id=1, source_target_pairs={{0,24},{4,28},{8,0},{12,4},{16,8},{20,12},{24,16},{28,20},{1,25},{... | collective-permute-start | bytes 786440 | tf_op jit(solution)/shard_map/ppermute | solution.py:113
  9.7 0.8 slice_bitcast_fusion.20
  10.5 4.8 %collective-permute-done.1 = f32[2,32,1024]{2,1,0:T(8,128)S(1)} collective-permute-done((f32[2,32,1024]{2,1,0:T(8,128)S(1)}, f32[2,32,1024]{2,1,0:T(8,128)S(1)}, u32[]{:S(2)}, u32[]{:S(2)}) %collective-permute-start.1) | collective-permute-done | bytes 262176 | tf_op jit(solution)/shard_map/ppermute | solution.py:113
  15.2 0.9 pad_maximum_fusion.5
  16.3 0.7 fusion.29
  16.9 0.9 constant_dynamic-update-slice_fusion.7
  17.9 0.2 select_reduce_fusion.3
  18.1 23.9 %collective-permute-done.2 = f32[2,32,2048]{2,1,0:T(8,128)S(1)} collective-permute-done((f32[2,32,2048]{2,1,0:T(8,128)S(1)}, f32[2,32,2048]{2,1,0:T(8,128)S(1)}, u32[]{:S(2)}, u32[]{:S(2)}) %collective-permute-start.2) | collective-permute-done | bytes 524320 | tf_op jit(solution)/shard_map/ppermute | solution.py:113
  42.3 0.3 copy.17
  42.6 0.3 copy.11
  42.9 0.6 gather_fusion
  43.5 1.9 %sine_bitcast_fusion.1 = (f32[32,8,512]{2,0,1:T(8,128)S(1)}, f32[32,8,512]{2,0,1:T(8,128)S(1)}) fusion(f32[8,32,512]{2,1,0:T(8,128)S(1)} %gather_fusion), kind=kLoop, calls=%fused_computation.50 | loop fusion | bytes 1572864 | tf_op jit(solution)/shard_map/sin | solution.py:89
  45.4 0.3 copy.12
  45.7 0.1 cos.57
  45.8 0.3 copy.13
  46.1 0.1 sin.57
  46.2 2.2 %multiply_subtract_fusion.1 = (f32[1,1,32,4096]{3,2,1,0:T(8,128)S(1)}, f32[1,1,32,4096]{3,2,1,0:T(8,128)S(1)}) fusion(f32[1,1,32,4096]{3,2,1,0:T(8,128)S(1)} %sin.57, f32[1,1,32,4096]{3,2,1,0:T(8,128)S(1)} %cos.57, f32[4096]{0:T(1024)S(1)} %fusion.24, f32[32]{0:T(128)S(1)} %fusion.29, pred[32]{0:T(512)(128)(4,1)S(1)} %compare_and_fusion), kind=kLoop, calls=%fused_computation.63 | loop fusion | flops 1310720 | bytes 2113696 | tf_op jit(solution)/shard_map/sub | solution.py:90
  48.4 0.9 fusion.13
  49.3 3.7 %collective-permute-start.3 = (f32[2,1,16,4096]{3,2,1,0:T(8,128)}, f32[2,1,16,4096]{3,2,1,0:T(8,128)}, u32[]{:S(2)}, u32[]{:S(2)}) collective-permute-start(f32[2,1,16,4096]{3,2,1,0:T(8,128)} %get-tuple-element.17), channel_id=1, source_target_pairs={{0,1},{1,2},{2,3},{4,5},{5,6},{6,7},{8,9},{9,10},{10,11},{12,13},{... | collective-permute-start | bytes 1572872 | tf_op jit(solution)/shard_map/ppermute | solution.py:20
  52.9 2.1 %collective-permute-start.4 = (f32[2,1,16,4096]{3,2,1,0:T(8,128)S(1)}, f32[2,1,16,4096]{3,2,1,0:T(8,128)}, u32[]{:S(2)}, u32[]{:S(2)}) collective-permute-start(f32[2,1,16,4096]{3,2,1,0:T(8,128)S(1)} %get-tuple-element.18), channel_id=1, source_target_pairs={{1,0},{2,1},{3,2},{5,4},{6,5},{7,6},{9,8},{10,9},{11,10},{13,12},{... | collective-permute-start | bytes 1572872 | tf_op jit(solution)/shard_map/ppermute | solution.py:22
  55.1 0.6 select_reduce_fusion.1
  55.6 0.3 copy.22
  55.9 0.3 copy.14
  56.3 0.6 gather_fusion.1
  56.8 1.9 %sine_bitcast_fusion = (f32[32,8,512]{2,0,1:T(8,128)S(1)}, f32[32,8,512]{2,0,1:T(8,128)S(1)}) fusion(f32[8,32,512]{2,1,0:T(8,128)S(1)} %gather_fusion.1), kind=kLoop, calls=%fused_computation.48 | loop fusion | bytes 1572864 | tf_op jit(solution)/shard_map/sin | solution.py:89
  58.7 0.3 copy.15
  59.0 0.1 cos.59
  59.1 0.3 copy.16
  59.6 4.0 %collective-permute-done.4 = f32[2,1,16,4096]{3,2,1,0:T(8,128)} collective-permute-done((f32[2,1,16,4096]{3,2,1,0:T(8,128)S(1)}, f32[2,1,16,4096]{3,2,1,0:T(8,128)}, u32[]{:S(2)}, u32[]{:S(2)}) %collective-permute-start.4) | collective-permute-done | bytes 524320 | tf_op jit(solution)/shard_map/ppermute | solution.py:22
  63.5 1.3 %pad_maximum_fusion = f32[2,1,64,4096]{3,2,1,0:T(8,128)S(1)} fusion(f32[2,1,16,4096]{3,2,1,0:T(8,128)} %collective-permute-done.4, f32[1,1,32,4096]{3,2,1,0:T(8,128)S(1)} %get-tuple-element.14, f32[1,1,32,4096]{3,2,1,0:T(8,128)S(1)} %get-tuple-element.13, f32[2,1,16,4096]{3,2,1,0:T(8,128)} %collective-permute-done.3), kind=kLoop, calls=%fused_computation.13 | loop fusion | flops 1572864 | bytes 4194304 | tf_op jit(solution)/shard_map/concatenate | solution.py:18
  64.9 0.7 fusion.5
  65.6 0.7 fusion.4
  66.3 0.7 fusion
  67.0 0.3 slice_bitcast_fusion.19
  67.5 0.7 fusion.1
  68.2 0.3 slice_bitcast_fusion.17
  68.7 1.0 fusion.11
  69.7 1.0 fusion.10
  70.7 1.8 %convolution_subtract_fusion.3 = f32[32,32,128]{2,1,0:T(8,128)} fusion(f32[32,32,128]{2,1,0:T(8,128)S(1)} %fusion.11, f32[1,32,32,32]{3,2,1,0:T(8,128)S(1)} %bitcast.154, f32[1,32,32,128]{3,2,1,0:T(8,128)S(1)} %bitcast.156, f32[160,128]{1,0:T(8,128)S(1)} %get-tuple-element.6), kind=kOutput, calls=%fused_computation.18 | convolution fusion | flops 251953152 | bytes 1785856 | tf_op jit(solution)/shard_map/...nj,jc->...nc/dot_general | solution.py:64
  72.5 1.1 %sub.181 = f32[1,1,32,4096]{3,2,1,0:T(8,128)S(1)} reshape(f32[32,32,128]{2,1,0:T(8,128)} %convolution_subtract_fusion.3) | data formatting | bytes 1048576 | tf_op jit(solution)/shard_map/sub | solution.py:68
  73.6 1.8 %convolution_add_fusion.3 = f32[32,32,128]{2,1,0:T(8,128)} fusion(f32[32,32,128]{2,1,0:T(8,128)S(1)} %fusion.10, f32[1,32,32,32]{3,2,1,0:T(8,128)S(1)} %bitcast.155, f32[1,32,32,128]{3,2,1,0:T(8,128)S(1)} %bitcast.157, f32[160,128]{1,0:T(8,128)S(1)} %get-tuple-element.5), kind=kOutput, calls=%fused_computation.17 | convolution fusion | flops 251953152 | bytes 1785856 | tf_op jit(solution)/shard_map/...nj,jc->...nc/dot_general | solution.py:64
  75.4 1.1 %add.196 = f32[1,1,32,4096]{3,2,1,0:T(8,128)S(1)} reshape(f32[32,32,128]{2,1,0:T(8,128)} %convolution_add_fusion.3) | data formatting | bytes 1048576 | tf_op jit(solution)/shard_map/add | solution.py:69
  76.5 0.1 multiply_subtract_fusion
  76.7 1.9 %collective-permute-start.5 = (f32[2,1,16,4096]{3,2,1,0:T(8,128)S(1)}, f32[2,1,16,4096]{3,2,1,0:T(8,128)S(1)}, u32[]{:S(2)}, u32[]{:S(2)}) collective-permute-start(f32[2,1,16,4096]{3,2,1,0:T(8,128)S(1)} %get-tuple-element.15), channel_id=1, source_target_pairs={{0,1},{1,2},{2,3},{4,5},{5,6},{6,7},{8,9},{9,10},{10,11},{12,13},{... | collective-permute-start | bytes 1572872 | tf_op jit(solution)/shard_map/ppermute | solution.py:20
  78.6 2.7 %collective-permute-start.6 = (f32[2,1,16,4096]{3,2,1,0:T(8,128)S(1)}, f32[2,1,16,4096]{3,2,1,0:T(8,128)S(1)}, u32[]{:S(2)}, u32[]{:S(2)}) collective-permute-start(f32[2,1,16,4096]{3,2,1,0:T(8,128)S(1)} %get-tuple-element.16), channel_id=1, source_target_pairs={{1,0},{2,1},{3,2},{5,4},{6,5},{7,6},{9,8},{10,9},{11,10},{13,12},{... | collective-permute-start | bytes 1572872 | tf_op jit(solution)/shard_map/ppermute | solution.py:22
  81.3 3.4 %collective-permute-done.5 = f32[2,1,16,4096]{3,2,1,0:T(8,128)S(1)} collective-permute-done((f32[2,1,16,4096]{3,2,1,0:T(8,128)S(1)}, f32[2,1,16,4096]{3,2,1,0:T(8,128)S(1)}, u32[]{:S(2)}, u32[]{:S(2)}) %collective-permute-start.5) | collective-permute-done | bytes 524320 | tf_op jit(solution)/shard_map/ppermute | solution.py:20
  84.7 4.4 %collective-permute-done.6 = f32[2,1,16,4096]{3,2,1,0:T(8,128)S(1)} collective-permute-done((f32[2,1,16,4096]{3,2,1,0:T(8,128)S(1)}, f32[2,1,16,4096]{3,2,1,0:T(8,128)S(1)}, u32[]{:S(2)}, u32[]{:S(2)}) %collective-permute-start.6) | collective-permute-done | bytes 524320 | tf_op jit(solution)/shard_map/ppermute | solution.py:22
  89.1 0.2 pad_maximum_fusion.1
  89.3 0.7 fusion.7
  90.0 0.7 fusion.6
  90.7 0.7 fusion.2
  91.4 0.3 slice_bitcast_fusion.15
  91.9 1.0 fusion.9
  92.9 1.0 fusion.8
  93.9 0.7 fusion.3
  94.6 0.3 slice_bitcast_fusion.13
  95.1 1.0 convolution_subtract_fusion.2
  96.2 1.0 convolution_add_fusion.2
  97.3 1.0 %pad_maximum_fusion.2 = f32[2,1,32,4096]{3,2,1,0:T(8,128)} fusion(f32[1,1,32,4096]{3,2,1,0:T(8,128)S(1)} %add.202, f32[1,1,32,4096]{3,2,1,0:T(8,128)S(1)} %sub.187), kind=kLoop, calls=%fused_computation.31 | loop fusion | flops 262144 | bytes 2097152 | tf_op jit(solution)/shard_map/stack | solution.py:136
  (29 shorter events, 1.5 us)
Async XLA Ops:
  0.0 42.1 %copy-start = (f32[2,32,512]{2,1,0:T(8,128)S(1)}, f32[2,32,512]{2,1,0:T(8,128)}, u32[]{:S(2)}) copy-start(f32[2,32,512]{2,1,0:T(8,128)} %param.6) | copy-start | bytes 393220
  0.0 7.8 %collective-permute-start = (f32[2,32,512]{2,1,0:T(8,128)}, f32[2,32,512]{2,1,0:T(8,128)S(1)}, u32[]{:S(2)}, u32[]{:S(2)}) collective-permute-start(f32[2,32,512]{2,1,0:T(8,128)} %param.6), channel_id=1, source_target_pairs={{0,28},{4,0},{8,4},{12,8},{16,12},{20,16},{24,20},{28,24},{1,29},{... | collective-permute-start | bytes 393224 | tf_op jit(solution)/shard_map/ppermute | solution.py:113
  8.7 6.5 %collective-permute-start.1 = (f32[2,32,1024]{2,1,0:T(8,128)S(1)}, f32[2,32,1024]{2,1,0:T(8,128)S(1)}, u32[]{:S(2)}, u32[]{:S(2)}) collective-permute-start(f32[2,32,1024]{2,1,0:T(8,128)S(1)} %pad_maximum_fusion.6), channel_id=1, source_target_pairs={{0,24},{4,28},{8,0},{12,4},{16,8},{20,12},{24,16},{28,20},{1,25},{... | collective-permute-start | bytes 786440 | tf_op jit(solution)/shard_map/ppermute | solution.py:113
  16.2 25.9 %collective-permute-start.2 = (f32[2,32,2048]{2,1,0:T(8,128)S(1)}, f32[2,32,2048]{2,1,0:T(8,128)S(1)}, u32[]{:S(2)}, u32[]{:S(2)}) collective-permute-start(f32[2,32,2048]{2,1,0:T(8,128)S(1)} %pad_maximum_fusion.5), channel_id=1, source_target_pairs={{0,16},{4,20},{8,24},{12,28},{16,0},{20,4},{24,8},{28,12},{1,17},{... | collective-permute-start | bytes 1572872 | tf_op jit(solution)/shard_map/ppermute | solution.py:113
  49.3 10.3 %collective-permute-start.3 = (f32[2,1,16,4096]{3,2,1,0:T(8,128)}, f32[2,1,16,4096]{3,2,1,0:T(8,128)}, u32[]{:S(2)}, u32[]{:S(2)}) collective-permute-start(f32[2,1,16,4096]{3,2,1,0:T(8,128)} %get-tuple-element.17), channel_id=1, source_target_pairs={{0,1},{1,2},{2,3},{4,5},{5,6},{6,7},{8,9},{9,10},{10,11},{12,13},{... | collective-permute-start | bytes 1572872 | tf_op jit(solution)/shard_map/ppermute | solution.py:20
  52.9 10.6 %collective-permute-start.4 = (f32[2,1,16,4096]{3,2,1,0:T(8,128)S(1)}, f32[2,1,16,4096]{3,2,1,0:T(8,128)}, u32[]{:S(2)}, u32[]{:S(2)}) collective-permute-start(f32[2,1,16,4096]{3,2,1,0:T(8,128)S(1)} %get-tuple-element.18), channel_id=1, source_target_pairs={{1,0},{2,1},{3,2},{5,4},{6,5},{7,6},{9,8},{10,9},{11,10},{13,12},{... | collective-permute-start | bytes 1572872 | tf_op jit(solution)/shard_map/ppermute | solution.py:22
  76.7 8.0 %collective-permute-start.5 = (f32[2,1,16,4096]{3,2,1,0:T(8,128)S(1)}, f32[2,1,16,4096]{3,2,1,0:T(8,128)S(1)}, u32[]{:S(2)}, u32[]{:S(2)}) collective-permute-start(f32[2,1,16,4096]{3,2,1,0:T(8,128)S(1)} %get-tuple-element.15), channel_id=1, source_target_pairs={{0,1},{1,2},{2,3},{4,5},{5,6},{6,7},{8,9},{9,10},{10,11},{12,13},{... | collective-permute-start | bytes 1572872 | tf_op jit(solution)/shard_map/ppermute | solution.py:20
  78.6 10.5 %collective-permute-start.6 = (f32[2,1,16,4096]{3,2,1,0:T(8,128)S(1)}, f32[2,1,16,4096]{3,2,1,0:T(8,128)S(1)}, u32[]{:S(2)}, u32[]{:S(2)}) collective-permute-start(f32[2,1,16,4096]{3,2,1,0:T(8,128)S(1)} %get-tuple-element.16), channel_id=1, source_target_pairs={{1,0},{2,1},{3,2},{5,4},{6,5},{7,6},{9,8},{10,9},{11,10},{13,12},{... | collective-permute-start | bytes 1572872 | tf_op jit(solution)/shard_map/ppermute | solution.py:22
